TPU v7x, 32 devices: a whole 2x2x4 slice. The times are simulated.
32 devices in a mesh: tile: 8 (over y, x, core), slab: 4 (over z).
Axes of the slice: x: 2, y: 2, z: 4, core: 2. Of those that a mesh axis runs over, the one named last changes fastest.
Arguments:
- estimate: float32 [64, 128, 512], P('slab', 'tile'), may hold values from 0.5 to 2
- observed: float32 [64, 128, 512], P('slab', 'tile'), may hold values from 0.25 to 4
- kernel_rows: float32 [31], replicated, may hold values from 0.001 to 1
- kernel_columns: float32 [31], replicated, may hold values from 0.001 to 1
- kernel_planes: float32 [31], replicated, may hold values from 0.001 to 1
Outputs:
- new_estimate: float32 [64, 128, 512], P('slab', 'tile')
- pyramid_level: float32 [64, 64, 256], P('slab', 'tile')
All inputs are finite; a program needn't handle non-finite values.
Results may differ from a plain program's by a relative error of at most 0.00005.
Values sent between devices are 32-bit elements; how exact they have to be, the bound alone decides.
No kernel may reach another device: no remote copies, remote signals or barrier semaphores. Data moves between devices by JAX's collectives and lax.ppermute only.
A program may use at most 64 MiB of HBM per device.

v0:
```python
import jax
import jax.numpy as jnp
from jax import lax
from jax.sharding import PartitionSpec as P

PRECISE = lax.Precision.HIGHEST


def extended(shard, sides, width):
    for axis, dim in sides:
        devices, length = (lax.axis_size(axis), shard.shape[dim])
        up = [(i, (i + 1) % devices) for i in range(devices - 1)]
        down = [(j, i) for i, j in up]
        last = lax.slice_in_dim(shard, length - width, length, axis=dim)
        initial = lax.slice_in_dim(shard, 0, width, axis=dim)
        before = lax.ppermute(last, axis, up)
        after = lax.ppermute(initial, axis, down)
        shard = jnp.concatenate([before, shard, after], axis=dim)
    return shard


def banded(kernel, row_count, col_count, orient, anchor):
    tap_count = kernel.shape[0]
    offset_index = (
        orient
        * (
            lax.broadcasted_iota(jnp.int32, (row_count, col_count), 0)
            - lax.broadcasted_iota(jnp.int32, (row_count, col_count), 1)
        )
        + anchor
    )
    inside = (offset_index >= 0) & (offset_index < tap_count)
    values = jnp.take(kernel, jnp.clip(offset_index, 0, tap_count - 1))
    return jnp.where(inside, values, jnp.zeros_like(values))


def pyramid_matrix(row_count, col_count, anchor):
    offset_index = (
        lax.broadcasted_iota(jnp.int32, (row_count, col_count), 0)
        - 2 * lax.broadcasted_iota(jnp.int32, (row_count, col_count), 1)
        + anchor
    )
    outer = (offset_index == 0) | (offset_index == 3)
    middle = (offset_index == 1) | (offset_index == 2)
    return jnp.where(
        outer, jnp.float32(0.125), jnp.where(middle, jnp.float32(0.375), jnp.float32(0.0))
    )


def across_depth(volume, matrix):
    return jnp.einsum("pxy,pq->qxy", volume, matrix, precision=PRECISE)


def across_rows(volume, matrix):
    return jnp.einsum("zpy,pq->zqy", volume, matrix, precision=PRECISE)


def across_columns(volume, matrix):
    return jnp.dot(volume, matrix, precision=PRECISE)


def shards(estimate, observed, kernel_rows, kernel_columns, kernel_planes):
    plane_count, row_count, col_count = estimate.shape
    reach_cells = (kernel_rows.shape[0] - 1) // 2
    groups = lax.axis_size("slab")
    planes_all = plane_count * groups
    padded = extended(estimate, (("tile", 1),), reach_cells)
    partial_value = across_rows(
        padded, banded(kernel_rows, row_count + 2 * reach_cells, row_count, 1, 0)
    )
    partial_value = across_columns(
        partial_value, banded(kernel_columns, col_count, col_count, 1, reach_cells)
    )
    forward_depth = banded(kernel_planes, planes_all, planes_all, 1, reach_cells)
    backward_depth = banded(kernel_planes, planes_all, planes_all, -1, reach_cells)
    turned = across_depth(
        lax.all_to_all(partial_value, "slab", split_axis=2, concat_axis=0, tiled=True),
        forward_depth,
    )
    blurred = lax.all_to_all(turned, "slab", split_axis=0, concat_axis=2, tiled=True)
    quotient = observed / blurred
    turned_back = across_depth(
        lax.all_to_all(quotient, "slab", split_axis=2, concat_axis=0, tiled=True), backward_depth
    )
    back_field = lax.all_to_all(turned_back, "slab", split_axis=0, concat_axis=2, tiled=True)
    spread = across_columns(
        back_field, banded(kernel_columns, col_count, col_count, -1, reach_cells)
    )
    padded_spread = extended(spread, (("tile", 1),), reach_cells)
    correction = across_rows(
        padded_spread,
        banded(kernel_rows, row_count + 2 * reach_cells, row_count, -1, 2 * reach_cells),
    )
    new_estimate = estimate * correction
    halved = across_columns(new_estimate, pyramid_matrix(col_count, col_count // 2, 1))
    padded_halved = extended(halved, (("tile", 1),), 1)
    pyramid_level = across_rows(padded_halved, pyramid_matrix(row_count + 2, row_count // 2, 0))
    return (new_estimate, pyramid_level)


def solution(mesh):
    in_specs = (P("slab", "tile", None), P("slab", "tile", None), P(), P(), P())
    out_specs = (P("slab", "tile", None), P("slab", "tile", None))
    return jax.shard_map(shards, mesh=mesh, in_specs=in_specs, out_specs=out_specs, check_vma=False)
```

profile of v0, /device:TPU:1, one launch (start us, length us, event | category | flops | bytes accessed | tf_op | source)
XLA Modules:
  0.0 230.6 jit_solution(3255726964246776414)
XLA Ops:
  0.7 1.3 fusion.571
  2.0 4.5 %collective-permute-start = (f32[16,15,512]{2,1,0:T(8,128)S(1)}, f32[16,15,512]{2,1,0:T(8,128)S(1)}, u32[]{:S(2)}, u32[]{:S(2)}) collective-permute-start(f32[16,15,512]{2,1,0:T(8,128)S(1)} %get-tuple-element.7), channel_id=1, source_target_pairs={{0,4},{4,8},{8,12},{12,16},{16,20},{20,24},{24,28},{1,5},{5,9},{9,... | collective-permute-start | bytes 1474568 | tf_op jit(solution)/shard_map/ppermute | solution.py:16
  6.5 1.9 collective-permute-start.1
  8.5 0.1 reshape.155
  8.6 4.8 %gather_fusion.3 = f32[736]{0:T(1024)S(1)} fusion(f32[31]{0:T(128)S(1)} %copy-done.1, s32[1024]{0:T(1024)S(1)} %pad_clamp_fusion), kind=kCustom, calls=%fused_computation.2.clone | custom fusion | bytes 8832 | tf_op jit(solution)/shard_map/jit(_take)/gather | solution.py:33
  13.5 0.7 fusion.574
  14.2 0.7 fusion.573
  14.9 5.0 %collective-permute-done.1 = f32[16,15,512]{2,1,0:T(8,128)S(1)} collective-permute-done((f32[16,15,512]{2,1,0:T(8,128)S(1)}, f32[16,15,512]{2,1,0:T(8,128)S(1)}, u32[]{:S(2)}, u32[]{:S(2)}) %collective-permute-start.1) | collective-permute-done | bytes 491552 | tf_op jit(solution)/shard_map/ppermute | solution.py:17
  19.9 1.0 fusion.15
  20.9 23.0 %fusion.23 = f32[16,16,512]{2,1,0:T(8,128)S(1)} fusion(f32[16,16,512]{2,1,0:T(8,128)S(1)} %fusion.15, f32[]{:T(128)} %bitcast.35, f32[]{:T(128)} %bitcast.34, f32[]{:T(128)} %bitcast.33, f32[]{:T(128)} %bitcast.32, f32[]{:T(128)} %bitcast.31, f32[]{:T(128)} %bitcast.30, f32[]{:T(128)} %bitcast.29, f32[]{:T(128)} %bitcast.28, f32[]{:T(128)} %bitcast.27, ...), kind=kOutput, calls=%fused_computation.25 | convolution fusion | flops 824705024 | bytes 1048700 | tf_op jit(solution)/shard_map/dot_general | solution.py:59
  43.9 3.6 %copy.19 = f32[16,16,512]{1,0,2:T(8,128)} copy(f32[16,16,512]{2,1,0:T(8,128)S(1)} %fusion.23) | data formatting | bytes 1048576 | tf_op jit(solution)/shard_map/dot_general | solution.py:59
  47.5 4.6 %reshape.229 = f32[4,1,32768]{2,1,0:T(1,128)} reshape(f32[512,16,16]{2,1,0:T(8,128)} %bitcast.121) | data formatting | bytes 1048576
  52.1 4.6 %all-to-all-start = ((f32[4,1,32768]{2,1,0:T(1,128)}), f32[4,1,32768]{2,1,0:T(1,128)S(1)}, u32[]{:S(2)}, u32[]{:S(2)}) async-start(f32[4,1,32768]{2,1,0:T(1,128)} %reshape.229), calls=%async_computation | async-start | bytes 1048576 | tf_op jit(solution)/shard_map/all_to_all | solution.py:77
  56.8 24.7 %gather_fusion.2 = f32[4096]{0:T(1024)S(1)} fusion(f32[31]{0:T(128)S(1)} %copy-done, s32[4096]{0:T(1024)S(1)} %broadcast_clamp_fusion), kind=kCustom, calls=%fused_computation.3.clone | custom fusion | bytes 49152 | tf_op jit(solution)/shard_map/jit(_take)/gather | solution.py:33
  81.6 0.5 broadcast.948
  82.1 2.1 reduce
  84.2 3.4 %reshape.230 = f32[512,16,16]{2,1,0:T(8,128)} reshape(f32[4,32768]{1,0:T(4,128)S(1)} %reduce) | data formatting | bytes 1048576
  87.7 3.3 %copy.20 = f32[16,16,4,128]{3,0,2,1:T(8,128)S(1)} copy(f32[16,16,4,128]{1,0,3,2:T(8,128)} %bitcast.122) | data formatting | bytes 1048576 | tf_op jit(solution)/shard_map/all_to_all | solution.py:77
  91.0 0.6 fusion.379
  91.7 1.1 copy.22
  92.8 4.5 %all-to-all-start.1 = ((f32[64,16,128]{2,1,0:T(8,128)}), f32[64,16,128]{2,1,0:T(8,128)S(1)}, u32[]{:S(2)}, u32[]{:S(2)}) async-start(f32[64,16,128]{2,1,0:T(8,128)} %copy.22), calls=%async_computation.1 | async-start | bytes 1048576 | tf_op jit(solution)/shard_map/all_to_all | solution.py:80
  97.3 3.7 %copy.24 = f32[16,16,512]{1,0,2:T(8,128)} copy(f32[16,16,512]{2,1,0:T(8,128)S(1)} %copy-done.3) | data formatting | bytes 1048576 | tf_op args[1]
  100.9 5.6 %all-to-all-done.1 = f32[64,16,128]{2,1,0:T(8,128)S(1)} async-done(((f32[64,16,128]{2,1,0:T(8,128)}), f32[64,16,128]{2,1,0:T(8,128)S(1)}, u32[]{:S(2)}, u32[]{:S(2)}) %all-to-all-start.1) | async-done | bytes 524320 | tf_op jit(solution)/shard_map/all_to_all | solution.py:80
  106.5 2.8 %copy.23 = f32[16,16,4,128]{1,0,3,2:T(8,128)} copy(f32[16,16,4,128]{3,1,0,2:T(8,128)S(1)} %bitcast.124) | data formatting | bytes 1048576 | tf_op jit(solution)/shard_map/all_to_all | solution.py:80
  109.3 6.0 %bitcast_divide_fusion = f32[16,16,512]{1,0,2:T(8,128)} fusion(f32[16,16,512]{1,0,2:T(8,128)} %copy.24, f32[16,16,4,128]{1,0,3,2:T(8,128)} %copy.23), kind=kLoop, calls=%fused_computation.4 | loop fusion | flops 131072 | bytes 1572864 | tf_op jit(solution)/shard_map/div | solution.py:81
  115.3 4.6 %reshape.231 = f32[4,1,32768]{2,1,0:T(1,128)} reshape(f32[512,16,16]{2,1,0:T(8,128)} %bitcast.120) | data formatting | bytes 1048576
  119.9 3.5 %all-to-all-start.2 = ((f32[4,1,32768]{2,1,0:T(1,128)}), f32[4,1,32768]{2,1,0:T(1,128)S(1)}, u32[]{:S(2)}, u32[]{:S(2)}) async-start(f32[4,1,32768]{2,1,0:T(1,128)} %reshape.231), calls=%async_computation.2 | async-start | bytes 1048576 | tf_op jit(solution)/shard_map/all_to_all | solution.py:83
  123.5 24.7 %gather_fusion.1 = f32[4096]{0:T(1024)S(1)} fusion(f32[31]{0:T(128)S(1)} %copy-done, s32[4096]{0:T(1024)S(1)} %broadcast_clamp_fusion.1), kind=kCustom, calls=%fused_computation.1.clone | custom fusion | bytes 49152 | tf_op jit(solution)/shard_map/jit(_take)/gather | solution.py:33
  148.3 2.1 reduce.1
  150.4 3.4 %reshape.232 = f32[512,16,16]{2,1,0:T(8,128)} reshape(f32[4,32768]{1,0:T(4,128)S(1)} %reduce.1) | data formatting | bytes 1048576
  153.8 3.3 %copy.25 = f32[16,16,4,128]{3,0,2,1:T(8,128)S(1)} copy(f32[16,16,4,128]{1,0,3,2:T(8,128)} %bitcast.123) | data formatting | bytes 1048576 | tf_op jit(solution)/shard_map/all_to_all | solution.py:83
  157.2 0.6 fusion.381
  157.8 0.3 copy.27
  158.1 15.2 %all_to_all.72 = f32[64,16,128]{2,1,0:T(8,128)S(1)} all-to-all(f32[64,16,128]{2,1,0:T(8,128)S(1)} %copy.27), channel_id=1, replica_groups=mesh['tile'=8,'slab'=4] {'slab'}, dimensions={0} | all-to-all | bytes 1048576 | tf_op jit(solution)/shard_map/all_to_all | solution.py:85
  173.4 0.3 copy.39
  173.7 0.2 all_to_all.67
  174.0 22.9 %fusion.21 = f32[16,16,512]{2,1,0:T(8,128)S(1)} fusion(f32[16,16,512]{2,1,0:T(8,128)S(1)} %all_to_all.67, f32[]{:T(128)} %bitcast.35, f32[]{:T(128)} %bitcast.34, f32[]{:T(128)} %bitcast.33, f32[]{:T(128)} %bitcast.32, f32[]{:T(128)} %bitcast.31, f32[]{:T(128)} %bitcast.30, f32[]{:T(128)} %bitcast.29, f32[]{:T(128)} %bitcast.28, f32[]{:T(128)} %bitcast.27, ...), kind=kOutput, calls=%fused_computation.23 | convolution fusion | flops 824967168 | bytes 1048700 | tf_op jit(solution)/shard_map/dot_general | solution.py:59
  196.9 0.1 fusion.570
  197.0 13.3 %collective-permute-start.2 = (f32[16,15,512]{2,1,0:T(8,128)S(1)}, f32[16,15,512]{2,1,0:T(8,128)S(1)}, u32[]{:S(2)}, u32[]{:S(2)}) collective-permute-start(f32[16,15,512]{2,1,0:T(8,128)S(1)} %get-tuple-element.4), channel_id=1, source_target_pairs={{0,4},{4,8},{8,12},{12,16},{16,20},{20,24},{24,28},{1,5},{5,9},{9,... | collective-permute-start | bytes 1474568 | tf_op jit(solution)/shard_map/ppermute | solution.py:16
  210.3 2.1 collective-permute-start.3
  212.5 4.8 %gather_fusion = f32[736]{0:T(1024)S(1)} fusion(f32[31]{0:T(128)S(1)} %copy-done.1, s32[1024]{0:T(1024)S(1)} %pad_clamp_fusion.1), kind=kCustom, calls=%fused_computation.clone | custom fusion | bytes 8832 | tf_op jit(solution)/shard_map/jit(_take)/gather | solution.py:33
  217.4 3.4 %collective-permute-done.3 = f32[16,15,512]{2,1,0:T(8,128)S(1)} collective-permute-done((f32[16,15,512]{2,1,0:T(8,128)S(1)}, f32[16,15,512]{2,1,0:T(8,128)S(1)}, u32[]{:S(2)}, u32[]{:S(2)}) %collective-permute-start.3) | collective-permute-done | bytes 491552 | tf_op jit(solution)/shard_map/ppermute | solution.py:17
  220.8 1.0 fusion.18
  221.8 0.7 fusion.223
  222.6 1.9 collective-permute-start.4
  224.5 2.4 %collective-permute-start.5 = (f32[16,1,256]{2,1,0:T(1,128)S(1)}, f32[16,1,256]{2,1,0:T(1,128)S(1)}, u32[]{:S(2)}, u32[]{:S(2)}) collective-permute-start(f32[16,1,256]{2,1,0:T(1,128)S(1)} %get-tuple-element.10), channel_id=1, source_target_pairs={{4,0},{8,4},{12,8},{16,12},{20,16},{24,20},{28,24},{5,1},{9,5},{13... | collective-permute-start | bytes 49160 | tf_op jit(solution)/shard_map/ppermute | solution.py:17
  226.9 2.6 %collective-permute-done.5 = f32[16,1,256]{2,1,0:T(1,128)S(1)} collective-permute-done((f32[16,1,256]{2,1,0:T(1,128)S(1)}, f32[16,1,256]{2,1,0:T(1,128)S(1)}, u32[]{:S(2)}, u32[]{:S(2)}) %collective-permute-start.5) | collective-permute-done | bytes 16416 | tf_op jit(solution)/shard_map/ppermute | solution.py:17
  229.6 1.0 convolution_bitcast_fusion
  (35 shorter events, 0.7 us)
Async XLA Ops:
  0.6 56.2 %copy-start = (f32[31]{0:T(128)S(1)}, f32[31]{0:T(128)}, u32[]{:S(2)}) copy-start(f32[31]{0:T(128)} %param.15) | copy-start | bytes 376
  0.6 7.9 %copy-start.1 = (f32[31]{0:T(128)S(1)}, f32[31]{0:T(128)}, u32[]{:S(2)}) copy-start(f32[31]{0:T(128)} %param.13) | copy-start | bytes 376
  2.0 12.9 %collective-permute-start = (f32[16,15,512]{2,1,0:T(8,128)S(1)}, f32[16,15,512]{2,1,0:T(8,128)S(1)}, u32[]{:S(2)}, u32[]{:S(2)}) collective-permute-start(f32[16,15,512]{2,1,0:T(8,128)S(1)} %get-tuple-element.7), channel_id=1, source_target_pairs={{0,4},{4,8},{8,12},{12,16},{16,20},{20,24},{24,28},{1,5},{5,9},{9,... | collective-permute-start | bytes 1474568 | tf_op jit(solution)/shard_map/ppermute | solution.py:16
  6.5 13.4 %collective-permute-start.1 = (f32[16,15,512]{2,1,0:T(8,128)S(1)}, f32[16,15,512]{2,1,0:T(8,128)S(1)}, u32[]{:S(2)}, u32[]{:S(2)}) collective-permute-start(f32[16,15,512]{2,1,0:T(8,128)S(1)} %get-tuple-element.8), channel_id=1, source_target_pairs={{4,0},{8,4},{12,8},{16,12},{20,16},{24,20},{28,24},{5,1},{9,5},{13... | collective-permute-start | bytes 1474568 | tf_op jit(solution)/shard_map/ppermute | solution.py:17
  8.6 4.9 %copy-start.5 = (f32[31]{0:T(128)S(1)}, f32[31]{0:T(128)}, u32[]{:S(2)}) copy-start(f32[31]{0:T(128)} %param.14) | copy-start | bytes 376
  8.6 11.3 %copy-start.2 = (f32[16,16,512]{2,1,0:T(8,128)S(1)}, f32[16,16,512]{2,1,0:T(8,128)}, u32[]{:S(2)}) copy-start(f32[16,16,512]{2,1,0:T(8,128)} %param.11) | copy-start | bytes 1572868
  52.1 29.5 %all-to-all-start = ((f32[4,1,32768]{2,1,0:T(1,128)}), f32[4,1,32768]{2,1,0:T(1,128)S(1)}, u32[]{:S(2)}, u32[]{:S(2)}) async-start(f32[4,1,32768]{2,1,0:T(1,128)} %reshape.229), calls=%async_computation | async-start | bytes 1048576 | tf_op jit(solution)/shard_map/all_to_all | solution.py:77
  91.0 6.3 %copy-start.3 = (f32[16,16,512]{2,1,0:T(8,128)S(1)}, f32[16,16,512]{2,1,0:T(8,128)}, u32[]{:S(2)}) copy-start(f32[16,16,512]{2,1,0:T(8,128)} %param.12) | copy-start | bytes 1572868
  92.8 13.7 %all-to-all-start.1 = ((f32[64,16,128]{2,1,0:T(8,128)}), f32[64,16,128]{2,1,0:T(8,128)S(1)}, u32[]{:S(2)}, u32[]{:S(2)}) async-start(f32[64,16,128]{2,1,0:T(8,128)} %copy.22), calls=%async_computation.1 | async-start | bytes 1048576 | tf_op jit(solution)/shard_map/all_to_all | solution.py:80
  119.9 28.4 %all-to-all-start.2 = ((f32[4,1,32768]{2,1,0:T(1,128)}), f32[4,1,32768]{2,1,0:T(1,128)S(1)}, u32[]{:S(2)}, u32[]{:S(2)}) async-start(f32[4,1,32768]{2,1,0:T(1,128)} %reshape.231), calls=%async_computation.2 | async-start | bytes 1048576 | tf_op jit(solution)/shard_map/all_to_all | solution.py:83
  197.0 20.4 %collective-permute-start.2 = (f32[16,15,512]{2,1,0:T(8,128)S(1)}, f32[16,15,512]{2,1,0:T(8,128)S(1)}, u32[]{:S(2)}, u32[]{:S(2)}) collective-permute-start(f32[16,15,512]{2,1,0:T(8,128)S(1)} %get-tuple-element.4), channel_id=1, source_target_pairs={{0,4},{4,8},{8,12},{12,16},{16,20},{20,24},{24,28},{1,5},{5,9},{9,... | collective-permute-start | bytes 1474568 | tf_op jit(solution)/shard_map/ppermute | solution.py:16
  210.3 10.5 %collective-permute-start.3 = (f32[16,15,512]{2,1,0:T(8,128)S(1)}, f32[16,15,512]{2,1,0:T(8,128)S(1)}, u32[]{:S(2)}, u32[]{:S(2)}) collective-permute-start(f32[16,15,512]{2,1,0:T(8,128)S(1)} %get-tuple-element.6), channel_id=1, source_target_pairs={{4,0},{8,4},{12,8},{16,12},{20,16},{24,20},{28,24},{5,1},{9,5},{13... | collective-permute-start | bytes 1474568 | tf_op jit(solution)/shard_map/ppermute | solution.py:17
  221.8 8.8 %copy-start.4 = (f32[16,16,512]{2,1,0:T(8,128)}, f32[16,16,512]{2,1,0:T(8,128)S(1)}, u32[]{:S(2)}) copy-start(f32[16,16,512]{2,1,0:T(8,128)S(1)} %fusion.18) | copy-start | bytes 1572868
  222.6 4.4 %collective-permute-start.4 = (f32[16,1,256]{2,1,0:T(1,128)S(1)}, f32[16,1,256]{2,1,0:T(1,128)S(1)}, u32[]{:S(2)}, u32[]{:S(2)}) collective-permute-start(f32[16,1,256]{2,1,0:T(1,128)S(1)} %get-tuple-element.9), channel_id=1, source_target_pairs={{0,4},{4,8},{8,12},{12,16},{16,20},{20,24},{24,28},{1,5},{5,9},{9,... | collective-permute-start | bytes 49160 | tf_op jit(solution)/shard_map/ppermute | solution.py:16
  224.5 5.1 %collective-permute-start.5 = (f32[16,1,256]{2,1,0:T(1,128)S(1)}, f32[16,1,256]{2,1,0:T(1,128)S(1)}, u32[]{:S(2)}, u32[]{:S(2)}) collective-permute-start(f32[16,1,256]{2,1,0:T(1,128)S(1)} %get-tuple-element.10), channel_id=1, source_target_pairs={{4,0},{8,4},{12,8},{16,12},{20,16},{24,20},{28,24},{5,1},{9,5},{13... | collective-permute-start | bytes 49160 | tf_op jit(solution)/shard_map/ppermute | solution.py:17
where the time goes:
time: 232 us; the launch traced here: 231 us
  local copies, waits for them, and re-layouts  97.8 us (42%)
  matrix products  50.9 us (22%)
  starting transfers between devices  38.8 us (17%)
  waiting for transfers between devices  16.6 us (7%)
  blocking collectives  15.2 us (7%)
  other arithmetic  10.3 us (4%)
    gather x10, local copies, waits for them, and re-layouts, banded(): values = jnp.take(kernel, jnp.clip(offset_index, 0, tap_count - 1))  60.7 us
    dot_general x3, matrix products, across_columns(): return jnp.dot(volume, matrix, precision=PRECISE)  46.6 us
    unnamed x17, local copies, waits for them, and re-layouts  19.8 us
    ppermute x3, starting transfers between devices, extended(): before = lax.ppermute(last, axis, up)  19.7 us
    all_to_all x1, blocking collectives, shards(): lax.all_to_all(turned_back, 'slab', split_axis=0, concat_axis=2, tiled=True)  15.2 us
    ppermute x3, waiting for transfers between devices, extended(): after = lax.ppermute(initial, axis, down)  11 us
    ppermute x3, starting transfers between devices, extended(): after = lax.ppermute(initial, axis, down)  6.46 us
    div x1, other arithmetic, shards(): quotient = observed / blurred  5.99 us
  transfers between devices with their start and end apart: 9, of which 4 were waited for; matrix products, arithmetic and copies ran while one was open for 28% of the time, Pallas kernels for 0%

commit v1 on v0

--- a/solution.py
+++ b/solution.py
@@ -82,7 +82,12 @@
     turned_back = across_depth(
         lax.all_to_all(quotient, "slab", split_axis=2, concat_axis=0, tiled=True), backward_depth
     )
-    back_field = lax.all_to_all(turned_back, "slab", split_axis=0, concat_axis=2, tiled=True)
+    back_field = jnp.concatenate(
+        lax.all_to_all(
+            jnp.stack(jnp.split(turned_back, lax.axis_size("slab"), axis=0)), "slab", 0, 0
+        ),
+        axis=2,
+    )
     spread = across_columns(
         back_field, banded(kernel_columns, col_count, col_count, -1, reach_cells)
     )

time: 232 us -> 232 us (level)
  no operation moved by 1% of the time
where the time goes in v1:
time: 232 us; the launch traced here: 230 us
  local copies, waits for them, and re-layouts  97.6 us (42%)
  matrix products  50.8 us (22%)
  starting transfers between devices  38.8 us (17%)
  waiting for transfers between devices  16.5 us (7%)
  blocking collectives  15.2 us (7%)
  other arithmetic  10.4 us (4%)
    gather x10, local copies, waits for them, and re-layouts, banded(): values = jnp.take(kernel, jnp.clip(offset_index, 0, tap_count - 1))  60.7 us
    dot_general x3, matrix products, across_columns(): return jnp.dot(volume, matrix, precision=PRECISE)  46.5 us
    unnamed x17, local copies, waits for them, and re-layouts  19.8 us
    ppermute x3, starting transfers between devices, extended(): before = lax.ppermute(last, axis, up)  19.7 us
    all_to_all x1, blocking collectives, shards(): lax.all_to_all(jnp.stack(jnp.split(turned_back, lax.axis_size('slab'), ax...  15.2 us
    ppermute x3, waiting for transfers between devices, extended(): after = lax.ppermute(initial, axis, down)  11 us
    ppermute x3, starting transfers between devices, extended(): after = lax.ppermute(initial, axis, down)  6.46 us
    div x1, other arithmetic, shards(): quotient = observed / blurred  6 us
  transfers between devices with their start and end apart: 9, of which 4 were waited for; matrix products, arithmetic and copies ran while one was open for 28% of the time, Pallas kernels for 0%

profile of v1, /device:TPU:1, one launch (start us, length us, event | category | flops | bytes accessed | tf_op | source)
XLA Modules:
  0.0 230.4 jit_solution(13871363637346014088)
XLA Ops:
  0.7 1.3 fusion.571
  2.0 4.5 %collective-permute-start = (f32[16,15,512]{2,1,0:T(8,128)S(1)}, f32[16,15,512]{2,1,0:T(8,128)S(1)}, u32[]{:S(2)}, u32[]{:S(2)}) collective-permute-start(f32[16,15,512]{2,1,0:T(8,128)S(1)} %get-tuple-element.11), channel_id=1, source_target_pairs={{0,4},{4,8},{8,12},{12,16},{16,20},{20,24},{24,28},{1,5},{5,9},{9,... | collective-permute-start | bytes 1474568 | tf_op jit(solution)/shard_map/ppermute | solution.py:16
  6.5 1.9 collective-permute-start.1
  8.5 0.1 reshape.163
  8.6 4.8 %gather_fusion.3 = f32[736]{0:T(1024)S(1)} fusion(f32[31]{0:T(128)S(1)} %copy-done.1, s32[1024]{0:T(1024)S(1)} %pad_clamp_fusion), kind=kCustom, calls=%fused_computation.2.clone | custom fusion | bytes 8832 | tf_op jit(solution)/shard_map/jit(_take)/gather | solution.py:33
  13.5 0.7 fusion.574
  14.2 0.7 fusion.573
  14.9 5.0 %collective-permute-done.1 = f32[16,15,512]{2,1,0:T(8,128)S(1)} collective-permute-done((f32[16,15,512]{2,1,0:T(8,128)S(1)}, f32[16,15,512]{2,1,0:T(8,128)S(1)}, u32[]{:S(2)}, u32[]{:S(2)}) %collective-permute-start.1) | collective-permute-done | bytes 491552 | tf_op jit(solution)/shard_map/ppermute | solution.py:17
  19.9 1.0 fusion.15
  20.9 22.9 %fusion.23 = f32[16,16,512]{2,1,0:T(8,128)S(1)} fusion(f32[16,16,512]{2,1,0:T(8,128)S(1)} %fusion.15, f32[]{:T(128)} %bitcast.35, f32[]{:T(128)} %bitcast.34, f32[]{:T(128)} %bitcast.33, f32[]{:T(128)} %bitcast.32, f32[]{:T(128)} %bitcast.31, f32[]{:T(128)} %bitcast.30, f32[]{:T(128)} %bitcast.29, f32[]{:T(128)} %bitcast.28, f32[]{:T(128)} %bitcast.27, ...), kind=kOutput, calls=%fused_computation.25 | convolution fusion | flops 824705024 | bytes 1048700 | tf_op jit(solution)/shard_map/dot_general | solution.py:59
  43.8 3.6 %copy.18 = f32[16,16,512]{1,0,2:T(8,128)} copy(f32[16,16,512]{2,1,0:T(8,128)S(1)} %fusion.23) | data formatting | bytes 1048576 | tf_op jit(solution)/shard_map/dot_general | solution.py:59
  47.5 4.6 %reshape.237 = f32[4,1,32768]{2,1,0:T(1,128)} reshape(f32[512,16,16]{2,1,0:T(8,128)} %bitcast.126) | data formatting | bytes 1048576
  52.1 4.6 %all-to-all-start = ((f32[4,1,32768]{2,1,0:T(1,128)}), f32[4,1,32768]{2,1,0:T(1,128)S(1)}, u32[]{:S(2)}, u32[]{:S(2)}) async-start(f32[4,1,32768]{2,1,0:T(1,128)} %reshape.237), calls=%async_computation | async-start | bytes 1048576 | tf_op jit(solution)/shard_map/all_to_all | solution.py:77
  56.8 24.7 %gather_fusion.2 = f32[4096]{0:T(1024)S(1)} fusion(f32[31]{0:T(128)S(1)} %copy-done, s32[4096]{0:T(1024)S(1)} %broadcast_clamp_fusion), kind=kCustom, calls=%fused_computation.3.clone | custom fusion | bytes 49152 | tf_op jit(solution)/shard_map/jit(_take)/gather | solution.py:33
  81.6 0.5 broadcast.948
  82.1 2.1 reduce
  84.2 3.4 %reshape.238 = f32[512,16,16]{2,1,0:T(8,128)} reshape(f32[4,32768]{1,0:T(4,128)S(1)} %reduce) | data formatting | bytes 1048576
  87.7 3.3 %copy.19 = f32[16,16,4,128]{3,0,2,1:T(8,128)S(1)} copy(f32[16,16,4,128]{1,0,3,2:T(8,128)} %bitcast.127) | data formatting | bytes 1048576 | tf_op jit(solution)/shard_map/all_to_all | solution.py:77
  91.0 0.6 fusion.379
  91.7 1.1 copy.21
  92.8 4.5 %all-to-all-start.1 = ((f32[64,16,128]{2,1,0:T(8,128)}), f32[64,16,128]{2,1,0:T(8,128)S(1)}, u32[]{:S(2)}, u32[]{:S(2)}) async-start(f32[64,16,128]{2,1,0:T(8,128)} %copy.21), calls=%async_computation.1 | async-start | bytes 1048576 | tf_op jit(solution)/shard_map/all_to_all | solution.py:80
  97.3 3.7 %copy.23 = f32[16,16,512]{1,0,2:T(8,128)} copy(f32[16,16,512]{2,1,0:T(8,128)S(1)} %copy-done.3) | data formatting | bytes 1048576 | tf_op args[1]
  101.0 5.5 %all-to-all-done.1 = f32[64,16,128]{2,1,0:T(8,128)S(1)} async-done(((f32[64,16,128]{2,1,0:T(8,128)}), f32[64,16,128]{2,1,0:T(8,128)S(1)}, u32[]{:S(2)}, u32[]{:S(2)}) %all-to-all-start.1) | async-done | bytes 524320 | tf_op jit(solution)/shard_map/all_to_all | solution.py:80
  106.5 2.8 %copy.22 = f32[16,16,4,128]{1,0,3,2:T(8,128)} copy(f32[16,16,4,128]{3,1,0,2:T(8,128)S(1)} %bitcast.129) | data formatting | bytes 1048576 | tf_op jit(solution)/shard_map/all_to_all | solution.py:80
  109.3 6.0 %bitcast_divide_fusion = f32[16,16,512]{1,0,2:T(8,128)} fusion(f32[16,16,512]{1,0,2:T(8,128)} %copy.23, f32[16,16,4,128]{1,0,3,2:T(8,128)} %copy.22), kind=kLoop, calls=%fused_computation.4 | loop fusion | flops 131072 | bytes 1572864 | tf_op jit(solution)/shard_map/div | solution.py:81
  115.3 4.6 %reshape.239 = f32[4,1,32768]{2,1,0:T(1,128)} reshape(f32[512,16,16]{2,1,0:T(8,128)} %bitcast.125) | data formatting | bytes 1048576
  120.0 3.5 %all-to-all-start.2 = ((f32[4,1,32768]{2,1,0:T(1,128)}), f32[4,1,32768]{2,1,0:T(1,128)S(1)}, u32[]{:S(2)}, u32[]{:S(2)}) async-start(f32[4,1,32768]{2,1,0:T(1,128)} %reshape.239), calls=%async_computation.2 | async-start | bytes 1048576 | tf_op jit(solution)/shard_map/all_to_all | solution.py:83
  123.5 24.7 %gather_fusion.1 = f32[4096]{0:T(1024)S(1)} fusion(f32[31]{0:T(128)S(1)} %copy-done, s32[4096]{0:T(1024)S(1)} %broadcast_clamp_fusion.1), kind=kCustom, calls=%fused_computation.1.clone | custom fusion | bytes 49152 | tf_op jit(solution)/shard_map/jit(_take)/gather | solution.py:33
  148.3 2.1 reduce.1
  150.5 3.4 %reshape.240 = f32[512,16,16]{2,1,0:T(8,128)} reshape(f32[4,32768]{1,0:T(4,128)S(1)} %reduce.1) | data formatting | bytes 1048576
  153.9 3.3 %copy.24 = f32[16,16,4,128]{3,0,2,1:T(8,128)S(1)} copy(f32[16,16,4,128]{1,0,3,2:T(8,128)} %bitcast.128) | data formatting | bytes 1048576 | tf_op jit(solution)/shard_map/all_to_all | solution.py:83
  157.2 0.6 fusion.381
  158.0 15.2 %all_to_all.59 = f32[4,16,16,128]{3,1,2,0:T(8,128)S(1)} all-to-all(f32[4,16,16,128]{3,1,2,0:T(8,128)S(1)} %pad_maximum_fusion), channel_id=1, replica_groups=mesh['tile'=8,'slab'=4] {'slab'}, dimensions={0} | all-to-all | bytes 1048576 | tf_op jit(solution)/shard_map/all_to_all | solution.py:86
  173.2 0.3 copy.26
  173.6 0.2 reshape.26
  173.8 22.9 %fusion.21 = f32[16,16,512]{2,1,0:T(8,128)S(1)} fusion(f32[16,16,512]{2,1,0:T(8,128)S(1)} %reshape.26, f32[]{:T(128)} %bitcast.35, f32[]{:T(128)} %bitcast.34, f32[]{:T(128)} %bitcast.33, f32[]{:T(128)} %bitcast.32, f32[]{:T(128)} %bitcast.31, f32[]{:T(128)} %bitcast.30, f32[]{:T(128)} %bitcast.29, f32[]{:T(128)} %bitcast.28, f32[]{:T(128)} %bitcast.27, ...), kind=kOutput, calls=%fused_computation.23 | convolution fusion | flops 824967168 | bytes 1048700 | tf_op jit(solution)/shard_map/dot_general | solution.py:59
  196.7 0.1 fusion.570
  196.8 13.3 %collective-permute-start.2 = (f32[16,15,512]{2,1,0:T(8,128)S(1)}, f32[16,15,512]{2,1,0:T(8,128)S(1)}, u32[]{:S(2)}, u32[]{:S(2)}) collective-permute-start(f32[16,15,512]{2,1,0:T(8,128)S(1)} %get-tuple-element.4), channel_id=1, source_target_pairs={{0,4},{4,8},{8,12},{12,16},{16,20},{20,24},{24,28},{1,5},{5,9},{9,... | collective-permute-start | bytes 1474568 | tf_op jit(solution)/shard_map/ppermute | solution.py:16
  210.1 2.1 collective-permute-start.3
  212.2 0.1 reshape.151
  212.3 4.8 %gather_fusion = f32[736]{0:T(1024)S(1)} fusion(f32[31]{0:T(128)S(1)} %copy-done.1, s32[1024]{0:T(1024)S(1)} %pad_clamp_fusion.1), kind=kCustom, calls=%fused_computation.clone | custom fusion | bytes 8832 | tf_op jit(solution)/shard_map/jit(_take)/gather | solution.py:33
  217.2 3.4 %collective-permute-done.3 = f32[16,15,512]{2,1,0:T(8,128)S(1)} collective-permute-done((f32[16,15,512]{2,1,0:T(8,128)S(1)}, f32[16,15,512]{2,1,0:T(8,128)S(1)}, u32[]{:S(2)}, u32[]{:S(2)}) %collective-permute-start.3) | collective-permute-done | bytes 491552 | tf_op jit(solution)/shard_map/ppermute | solution.py:17
  220.6 1.0 fusion.18
  221.6 0.7 fusion.223
  222.3 1.9 collective-permute-start.4
  224.3 2.4 %collective-permute-start.5 = (f32[16,1,256]{2,1,0:T(1,128)S(1)}, f32[16,1,256]{2,1,0:T(1,128)S(1)}, u32[]{:S(2)}, u32[]{:S(2)}) collective-permute-start(f32[16,1,256]{2,1,0:T(1,128)S(1)} %get-tuple-element.14), channel_id=1, source_target_pairs={{4,0},{8,4},{12,8},{16,12},{20,16},{24,20},{28,24},{5,1},{9,5},{13... | collective-permute-start | bytes 49160 | tf_op jit(solution)/shard_map/ppermute | solution.py:17
  226.7 2.6 %collective-permute-done.5 = f32[16,1,256]{2,1,0:T(1,128)S(1)} collective-permute-done((f32[16,1,256]{2,1,0:T(1,128)S(1)}, f32[16,1,256]{2,1,0:T(1,128)S(1)}, u32[]{:S(2)}, u32[]{:S(2)}) %collective-permute-start.5) | collective-permute-done | bytes 16416 | tf_op jit(solution)/shard_map/ppermute | solution.py:17
  229.3 1.0 convolution_bitcast_fusion
  (36 shorter events, 0.7 us)
Async XLA Ops:
  0.6 56.1 %copy-start = (f32[31]{0:T(128)S(1)}, f32[31]{0:T(128)}, u32[]{:S(2)}) copy-start(f32[31]{0:T(128)} %param.15) | copy-start | bytes 376
  0.6 7.9 %copy-start.1 = (f32[31]{0:T(128)S(1)}, f32[31]{0:T(128)}, u32[]{:S(2)}) copy-start(f32[31]{0:T(128)} %param.13) | copy-start | bytes 376
  2.0 12.9 %collective-permute-start = (f32[16,15,512]{2,1,0:T(8,128)S(1)}, f32[16,15,512]{2,1,0:T(8,128)S(1)}, u32[]{:S(2)}, u32[]{:S(2)}) collective-permute-start(f32[16,15,512]{2,1,0:T(8,128)S(1)} %get-tuple-element.11), channel_id=1, source_target_pairs={{0,4},{4,8},{8,12},{12,16},{16,20},{20,24},{24,28},{1,5},{5,9},{9,... | collective-permute-start | bytes 1474568 | tf_op jit(solution)/shard_map/ppermute | solution.py:16
  6.5 13.4 %collective-permute-start.1 = (f32[16,15,512]{2,1,0:T(8,128)S(1)}, f32[16,15,512]{2,1,0:T(8,128)S(1)}, u32[]{:S(2)}, u32[]{:S(2)}) collective-permute-start(f32[16,15,512]{2,1,0:T(8,128)S(1)} %get-tuple-element.12), channel_id=1, source_target_pairs={{4,0},{8,4},{12,8},{16,12},{20,16},{24,20},{28,24},{5,1},{9,5},{13... | collective-permute-start | bytes 1474568 | tf_op jit(solution)/shard_map/ppermute | solution.py:17
  8.6 4.9 %copy-start.5 = (f32[31]{0:T(128)S(1)}, f32[31]{0:T(128)}, u32[]{:S(2)}) copy-start(f32[31]{0:T(128)} %param.14) | copy-start | bytes 376
  8.6 11.3 %copy-start.2 = (f32[16,16,512]{2,1,0:T(8,128)S(1)}, f32[16,16,512]{2,1,0:T(8,128)}, u32[]{:S(2)}) copy-start(f32[16,16,512]{2,1,0:T(8,128)} %param.11) | copy-start | bytes 1572868
  52.1 29.5 %all-to-all-start = ((f32[4,1,32768]{2,1,0:T(1,128)}), f32[4,1,32768]{2,1,0:T(1,128)S(1)}, u32[]{:S(2)}, u32[]{:S(2)}) async-start(f32[4,1,32768]{2,1,0:T(1,128)} %reshape.237), calls=%async_computation | async-start | bytes 1048576 | tf_op jit(solution)/shard_map/all_to_all | solution.py:77
  91.0 6.3 %copy-start.3 = (f32[16,16,512]{2,1,0:T(8,128)S(1)}, f32[16,16,512]{2,1,0:T(8,128)}, u32[]{:S(2)}) copy-start(f32[16,16,512]{2,1,0:T(8,128)} %param.12) | copy-start | bytes 1572868
  92.8 13.7 %all-to-all-start.1 = ((f32[64,16,128]{2,1,0:T(8,128)}), f32[64,16,128]{2,1,0:T(8,128)S(1)}, u32[]{:S(2)}, u32[]{:S(2)}) async-start(f32[64,16,128]{2,1,0:T(8,128)} %copy.21), calls=%async_computation.1 | async-start | bytes 1048576 | tf_op jit(solution)/shard_map/all_to_all | solution.py:80
  120.0 28.4 %all-to-all-start.2 = ((f32[4,1,32768]{2,1,0:T(1,128)}), f32[4,1,32768]{2,1,0:T(1,128)S(1)}, u32[]{:S(2)}, u32[]{:S(2)}) async-start(f32[4,1,32768]{2,1,0:T(1,128)} %reshape.239), calls=%async_computation.2 | async-start | bytes 1048576 | tf_op jit(solution)/shard_map/all_to_all | solution.py:83
  196.8 20.4 %collective-permute-start.2 = (f32[16,15,512]{2,1,0:T(8,128)S(1)}, f32[16,15,512]{2,1,0:T(8,128)S(1)}, u32[]{:S(2)}, u32[]{:S(2)}) collective-permute-start(f32[16,15,512]{2,1,0:T(8,128)S(1)} %get-tuple-element.4), channel_id=1, source_target_pairs={{0,4},{4,8},{8,12},{12,16},{16,20},{20,24},{24,28},{1,5},{5,9},{9,... | collective-permute-start | bytes 1474568 | tf_op jit(solution)/shard_map/ppermute | solution.py:16
  210.1 10.5 %collective-permute-start.3 = (f32[16,15,512]{2,1,0:T(8,128)S(1)}, f32[16,15,512]{2,1,0:T(8,128)S(1)}, u32[]{:S(2)}, u32[]{:S(2)}) collective-permute-start(f32[16,15,512]{2,1,0:T(8,128)S(1)} %get-tuple-element.6), channel_id=1, source_target_pairs={{4,0},{8,4},{12,8},{16,12},{20,16},{24,20},{28,24},{5,1},{9,5},{13... | collective-permute-start | bytes 1474568 | tf_op jit(solution)/shard_map/ppermute | solution.py:17
  221.6 8.8 %copy-start.4 = (f32[16,16,512]{2,1,0:T(8,128)}, f32[16,16,512]{2,1,0:T(8,128)S(1)}, u32[]{:S(2)}) copy-start(f32[16,16,512]{2,1,0:T(8,128)S(1)} %fusion.18) | copy-start | bytes 1572868
  222.3 4.4 %collective-permute-start.4 = (f32[16,1,256]{2,1,0:T(1,128)S(1)}, f32[16,1,256]{2,1,0:T(1,128)S(1)}, u32[]{:S(2)}, u32[]{:S(2)}) collective-permute-start(f32[16,1,256]{2,1,0:T(1,128)S(1)} %get-tuple-element.13), channel_id=1, source_target_pairs={{0,4},{4,8},{8,12},{12,16},{16,20},{20,24},{24,28},{1,5},{5,9},{9,... | collective-permute-start | bytes 49160 | tf_op jit(solution)/shard_map/ppermute | solution.py:16
  224.3 5.1 %collective-permute-start.5 = (f32[16,1,256]{2,1,0:T(1,128)S(1)}, f32[16,1,256]{2,1,0:T(1,128)S(1)}, u32[]{:S(2)}, u32[]{:S(2)}) collective-permute-start(f32[16,1,256]{2,1,0:T(1,128)S(1)} %get-tuple-element.14), channel_id=1, source_target_pairs={{4,0},{8,4},{12,8},{16,12},{20,16},{24,20},{28,24},{5,1},{9,5},{13... | collective-permute-start | bytes 49160 | tf_op jit(solution)/shard_map/ppermute | solution.py:17
